TPU v7x, 128 devices: a whole 4x4x4 slice. The times are simulated.
128 devices in a mesh: row: 16 (over y, x_hi, core), col: 8 (over x_lo, z).
Axes of the slice: x: 4 (x_hi: 2, x_lo: 2; x = x_hi * 2 + x_lo), y: 4, z: 4, core: 2. Of those that a mesh axis runs over, the one named last changes fastest.
Arguments:
- matrix: float32 [24576, 4, 3072], P('row', None, 'col'), may hold values from -60 to 60, as said below
Outputs:
- factored: float32 [24576, 4, 3072], P('row', None, 'col')
- r_rows: float32 [2, 384, 4, 3072], P(None, None, None, 'col')
Inputs may be any that keep to these rules, and one draw needn't show every extreme that they name: `matrix`: dense real entries with column scales that differ from column to column.
All inputs are finite; a program needn't handle non-finite values.
Results may differ from a plain program's by a relative error of at most 0.00017.
Values sent between devices are 32-bit elements; how exact they have to be, the bound alone decides.
No kernel may reach another device: no remote copies, remote signals or barrier semaphores. Data moves between devices by JAX's collectives and lax.ppermute only.
A program may use at most 128 MiB of HBM per device.

v0:
```python
import jax
import jax.numpy as jnp
from jax import lax
from jax.sharding import PartitionSpec as P

STEPS = 2


def spread(block, axis, holder):
    block = jnp.where(lax.axis_index(axis) == holder, block, jnp.zeros_like(block))
    return lax.psum(block, axis)


def shards(matrix):
    highest = lax.Precision.HIGHEST
    ncol = lax.axis_size("col")
    column = lax.axis_index("col")
    count = matrix.shape[1]
    width = matrix.shape[2]
    glob = jnp.arange(count, dtype=jnp.int32) * ncol + column
    ident = jnp.eye(width, dtype=jnp.float32)
    blocks = matrix
    rows_out = []
    for k in range(STEPS):
        owner = k % ncol
        local_index = k // ncol
        local_panel = blocks[:, local_index, :]
        gram = lax.psum(
            jnp.dot(
                local_panel.T, local_panel, precision=highest, preferred_element_type=jnp.float32
            ),
            "row",
        )
        lower = jnp.linalg.cholesky(gram)
        inverse = lax.linalg.triangular_solve(lower, ident, left_side=True, lower=True)
        own_basis = jnp.dot(
            local_panel, inverse.T, precision=highest, preferred_element_type=jnp.float32
        )
        basis = spread(own_basis, "col", owner)
        partial_proj = jnp.einsum("mb,mjt->bjt", basis, blocks, precision=highest)
        proj = lax.psum(partial_proj, "row")
        kept = jnp.where((glob > k)[None, :, None], proj, jnp.float32(0.0))
        blocks = blocks - jnp.einsum("mb,bjt->mjt", basis, kept, precision=highest)
        is_panel = (glob == k)[None, :, None]
        blocks = jnp.where(is_panel, basis[:, None, :], blocks)
        rows_out.append(jnp.where(is_panel, lower.T[:, None, :], kept))
    return (blocks, jnp.stack(rows_out))


def solution(mesh):
    return jax.shard_map(
        shards,
        mesh=mesh,
        in_specs=(P("row", None, "col"),),
        out_specs=(P("row", None, "col"), P(None, None, None, "col")),
        check_vma=False,
    )
```

profile of v0, /device:TPU:0, one launch (start us, length us, event | category | flops | bytes accessed | tf_op | source)
XLA Modules:
  0.0 1087.4 jit_solution(16035788120656499901)
XLA Ops:
  7.2 4.3 copy.16
  11.5 3.7 copy-done.1
  15.2 4.8 fusion.7
  20.7 141.6 %all-reduce.8.cloned.1.call-done = f32[384,384]{0,1:T(8,128)} async-done(((f32[384,384]{0,1:T(8,128)}), f32[384,384]{0,1:T(8,128)}) %all-reduce.8.cloned.1.call-update) | async-done | bytes 589840 | tf_op jit(solution)/shard_map/psum | solution.py:28
  162.3 1.3 copy.18
  163.6 1.1 fusion.26
  164.7 11.7 %cholesky.208 = f32[128,128]{1,0:T(8,128)S(1)} custom-call(f32[128,128]{1,0:T(8,128)S(1)} %cholesky.310), custom_call_target="Cholesky" | custom-call | tf_op jit(solution)/shard_map/jit(cholesky)/cholesky | solution.py:34
  176.4 9.8 custom-call.20
  186.9 11.7 %cholesky.227 = f32[128,128]{1,0:T(8,128)S(1)} custom-call(f32[128,128]{1,0:T(8,128)S(1)} %cholesky.314), custom_call_target="Cholesky" | custom-call | tf_op jit(solution)/shard_map/jit(cholesky)/cholesky | solution.py:34
  198.6 10.0 custom-call.21
  209.1 11.7 %cholesky.246 = f32[128,128]{1,0:T(8,128)S(1)} custom-call(f32[128,128]{1,0:T(8,128)S(1)} %convolution_subtract_fusion.7), custom_call_target="Cholesky" | custom-call | tf_op jit(solution)/shard_map/jit(cholesky)/cholesky | solution.py:34
  224.2 6.4 while.4
  224.9 1.4 bitcast_dynamic-update-slice_fusion.4
  227.0 1.4 bitcast_dynamic-update-slice_fusion.4
  229.1 1.4 bitcast_dynamic-update-slice_fusion.4
  230.6 29.5 %custom-call.22 = f32[3,128,128]{1,2,0:T(8,128)S(1)} custom-call(f32[3,128,128]{2,1,0:T(8,128)S(1)} %get-tuple-element.18), custom_call_target="InvertDiagBlocksLowerTriangular" | custom-call | tf_op jit(solution)/shard_map/triangular_solve/custom-call.2 | solution.py:35
  261.9 7.0 fusion
  269.0 81.4 %all-reduce.10.cloned.1.call-done = f32[1536,384]{0,1:T(8,128)} async-done(((f32[1536,384]{0,1:T(8,128)}), f32[1536,384]{0,1:T(8,128)}) %all-reduce.10.cloned.1.call-update) | async-done | bytes 2359312 | tf_op jit(solution)/shard_map/psum | solution.py:11
  350.4 16.7 %fusion.4 = f32[384,4,384]{2,0,1:T(8,128)} fusion(f32[1536,384]{0,1:T(8,128)} %all-reduce.10.cloned.1.call-done, f32[1536,4,384]{2,1,0:T(4,128)} %param.4), kind=kOutput, calls=%fused_computation.15 | convolution fusion | flops 10871635968 | bytes 14155776 | tf_op jit(solution)/shard_map/mb,mjt->bjt/dot_general | solution.py:40
  367.2 2.0 copy.19
  369.3 145.5 %all-reduce.12.cloned.1.call-done = f32[384,4,384]{2,0,1:T(8,128)} async-done(((f32[384,4,384]{2,0,1:T(8,128)}), f32[384,4,384]{2,0,1:T(8,128)}) %all-reduce.12.cloned.1.call-update) | async-done | bytes 2359312 | tf_op jit(solution)/shard_map/psum | solution.py:41
  514.8 21.5 %subtract_select_fusion.1 = f32[1536,4,384]{2,0,1:T(8,128)S(1)} fusion(f32[1536,384]{1,0:T(8,128)S(1)} %copy.19, pred[4]{0:T(512)(128)(4,1)S(1)} %get-tuple-element.67, f32[1536,384]{0,1:T(8,128)} %all-reduce.10.cloned.1.call-done, f32[384,4,384]{2,0,1:T(8,128)} %all-reduce.12.cloned.1.call-done, pred[4]{0:T(512)(128)(4,1)S(1)} %get-tuple-element.66, ...), kind=kOutput, calls=%fused_computation.5 | convolution fusion | flops 10876944384 | bytes 25952264 | tf_op jit(solution)/shard_map/mb,bjt->mjt/dot_general | solution.py:43
  536.4 3.7 copy-done
  540.1 4.8 fusion.8
  545.0 139.8 %all-reduce.14.cloned.1.call-done = f32[384,384]{0,1:T(8,128)} async-done(((f32[384,384]{0,1:T(8,128)}), f32[384,384]{0,1:T(8,128)}) %all-reduce.14.cloned.1.call-update) | async-done | bytes 589840 | tf_op jit(solution)/shard_map/psum | solution.py:28
  684.8 1.3 copy.24
  686.1 1.1 fusion.25
  687.3 11.7 %cholesky.261 = f32[128,128]{1,0:T(8,128)S(1)} custom-call(f32[128,128]{1,0:T(8,128)S(1)} %cholesky.318), custom_call_target="Cholesky" | custom-call | tf_op jit(solution)/shard_map/jit(cholesky)/cholesky | solution.py:34
  699.7 9.8 custom-call.23
  710.1 11.7 %cholesky.280 = f32[128,128]{1,0:T(8,128)S(1)} custom-call(f32[128,128]{1,0:T(8,128)S(1)} %cholesky.322), custom_call_target="Cholesky" | custom-call | tf_op jit(solution)/shard_map/jit(cholesky)/cholesky | solution.py:34
  722.5 10.2 custom-call.24
  733.2 11.7 %cholesky.299 = f32[128,128]{1,0:T(8,128)S(1)} custom-call(f32[128,128]{1,0:T(8,128)S(1)} %convolution_subtract_fusion.6), custom_call_target="Cholesky" | custom-call | tf_op jit(solution)/shard_map/jit(cholesky)/cholesky | solution.py:34
  748.3 6.1 while.5
  749.0 1.4 bitcast_dynamic-update-slice_fusion.5
  751.0 1.4 bitcast_dynamic-update-slice_fusion.5
  753.1 1.4 bitcast_dynamic-update-slice_fusion.5
  754.5 29.5 %custom-call.25 = f32[3,128,128]{1,2,0:T(8,128)S(1)} custom-call(f32[3,128,128]{2,1,0:T(8,128)S(1)} %get-tuple-element.19), custom_call_target="InvertDiagBlocksLowerTriangular" | custom-call | tf_op jit(solution)/shard_map/triangular_solve/custom-call.2 | solution.py:35
  785.8 6.9 convolution_select_fusion
  792.8 81.4 %all-reduce.16.cloned.1.call-done = f32[1536,384]{1,0:T(8,128)} async-done(((f32[1536,384]{1,0:T(8,128)}), f32[1536,384]{1,0:T(8,128)}) %all-reduce.16.cloned.1.call-update) | async-done | bytes 2359312 | tf_op jit(solution)/shard_map/psum | solution.py:11
  874.2 16.2 %fusion.1 = f32[384,4,384]{2,0,1:T(8,128)} fusion(f32[1536,4,384]{2,0,1:T(8,128)} %copy-done, f32[1536,384]{1,0:T(8,128)} %all-reduce.16.cloned.1.call-done), kind=kOutput, calls=%fused_computation.12 | convolution fusion | flops 10871635968 | bytes 14155776 | tf_op jit(solution)/shard_map/mb,mjt->bjt/dot_general | solution.py:40
  890.5 1.0 copy.26
  892.3 2.8 select_bitcast_fusion.1
  895.3 142.8 %all-reduce.18.cloned.1.call-done = f32[384,4,384]{2,0,1:T(8,128)} async-done(((f32[384,4,384]{2,0,1:T(8,128)}), f32[384,4,384]{2,0,1:T(8,128)}) %all-reduce.18.cloned.1.call-update) | async-done | bytes 2359312 | tf_op jit(solution)/shard_map/psum | solution.py:41
  1038.1 2.1 select_bitcast_fusion
  1040.8 5.4 copy.29
  1046.3 1.1 copy-done.4
  1047.4 16.5 %subtract_select_fusion = f32[1536,4,384]{2,0,1:T(8,128)S(1)} fusion(f32[1536,4,384]{2,0,1:T(8,128)S(1)} %bitcast.110, f32[1536,384]{1,0:T(8,128)S(1)} %copy-done.2, pred[4]{0:T(512)(128)(4,1)S(1)} %get-tuple-element.69, f32[384,4,384]{2,0,1:T(8,128)S(1)} %copy-done.4, pred[4]{0:T(512)(128)(4,1)S(1)} %get-tuple-element.68), kind=kOutput, calls=%fused_computation.4 | convolution fusion | flops 10876944384 | bytes 23592968 | tf_op jit(solution)/shard_map/mb,bjt->mjt/dot_general | solution.py:43
  1063.9 16.5 %copy.28 = f32[1536,4,384]{2,1,0:T(4,128)} copy(f32[1536,4,384]{2,0,1:T(8,128)S(1)} %subtract_select_fusion) | data formatting | bytes 18874368
  (88 shorter events, 16.8 us)
Async XLA Ops:
  7.2 155.1 %all-reduce.8.cloned.1.call-start = ((), (), s32[]{:S(2)}) async-start(), calls=%async_computation | async-start | bytes 1179648 | tf_op jit(solution)/shard_map/psum | solution.py:28
  11.5 3.7 copy-start.1
  20.1 330.3 %all-reduce.10.cloned.1.call-start = ((), (), s32[]{:S(2)}) async-start(), calls=%async_computation.1 | async-start | bytes 4718592 | tf_op jit(solution)/shard_map/psum | solution.py:11
  268.9 245.9 %all-reduce.12.cloned.1.call-start = ((), (), s32[]{:S(2)}) async-start(), calls=%async_computation.2 | async-start | bytes 4718592 | tf_op jit(solution)/shard_map/psum | solution.py:41
  367.2 317.7 %all-reduce.14.cloned.1.call-start = ((), (), s32[]{:S(2)}) async-start(), calls=%async_computation.3 | async-start | bytes 1179648 | tf_op jit(solution)/shard_map/psum | solution.py:28
  536.4 3.7 copy-start
  545.0 329.2 %all-reduce.16.cloned.1.call-start = ((), (), s32[]{:S(2)}) async-start(), calls=%async_computation.4 | async-start | bytes 4718592 | tf_op jit(solution)/shard_map/psum | solution.py:11
  792.8 245.4 %all-reduce.18.cloned.1.call-start = ((), (), s32[]{:S(2)}) async-start(), calls=%async_computation.5 | async-start | bytes 4718592 | tf_op jit(solution)/shard_map/psum | solution.py:41
  890.4 1.9 copy-start.3
  892.3 2.8 copy-start.6
  1038.1 2.4 copy-start.5
  1040.5 5.8 slice-start
  1040.5 5.8 slice-start.1
  1040.8 5.5 slice-start.2
  1040.8 5.5 copy-start.2
  1040.8 6.6 copy-start.4
Sparse Core Ops, SparseCore 0:
  20.2 141.9 all-reduce.7
  269.1 81.3 all-reduce.9
  367.3 147.4 all-reduce.11
  545.1 139.7 all-reduce.13
  792.9 81.2 all-reduce.15
  890.6 147.5 all-reduce.17
where the time goes:
time: 1090 us
  waiting for transfers between devices  733 us (67%)
  other arithmetic  181 us (17%)
  matrix products  100 us (9%)
  local copies, waits for them, and re-layouts  54.3 us (5%)
  between operations  18.5 us (2%)
    psum x2, waiting for transfers between devices, shards(): proj = lax.psum(partial_proj, 'row')  288 us
    psum x2, waiting for transfers between devices, shards(): lax.psum(jnp.dot(local_panel.T, local_panel, precision=highest, preferred...  281 us
    psum x2, waiting for transfers between devices, spread(): return lax.psum(block, axis)  163 us
    another operation x21, other arithmetic, shards(): lower = jnp.linalg.cholesky(gram)  114 us
    another operation x3, other arithmetic, shards(): lax.linalg.triangular_solve(lower, ident, left_side=True, lower=True)  59 us
    dot_general x2, matrix products, shards(): blocks = blocks - jnp.einsum('mb,bjt->mjt', basis, kept, precision=highest)  38 us
    unnamed x23, local copies, waits for them, and re-layouts  35.9 us
    dot_general x2, matrix products, shards(): partial_proj = jnp.einsum('mb,mjt->bjt', basis, blocks, precision=highest)  32.9 us
  transfers between devices with their start and end apart: 6, of which 6 were waited for; matrix products, arithmetic and copies ran while one was open for 1% of the time, Pallas kernels for 0%

commit v1 on v0

--- a/solution.py
+++ b/solution.py
@@ -8,7 +8,8 @@
 
 def spread(block, axis, holder):
     block = jnp.where(lax.axis_index(axis) == holder, block, jnp.zeros_like(block))
-    return lax.psum(block, axis)
+    supply_the_corner = lambda local, group_axis: jnp.sum(lax.all_gather(local, group_axis), axis=0)
+    return supply_the_corner(block, axis)
 
 
 def shards(matrix):

time: 1090 us -> 1330 us (1.22)
  waiting for transfers between devices: 733 us -> 943 us
  local copies, waits for them, and re-layouts: 54.3 us -> 74 us
    all_gather x0 -> x2, waiting for transfers between devices: none -> 376 us  [spread(): lax.all_gather(local, group_axis)]
    psum x2 -> x0, waiting for transfers between devices: 163 us -> none  [spread(): return lax.psum(block, axis)]
    unnamed x23 -> x28, local copies, waits for them, and re-layouts: 35.9 us -> 55.2 us
where the time goes in v1:
time: 1330 us
  waiting for transfers between devices  943 us (71%)
  other arithmetic  194 us (15%)
  matrix products  95.8 us (7%)
  local copies, waits for them, and re-layouts  74 us (6%)
  between operations  18.7 us (1%)
    all_gather x2, waiting for transfers between devices, spread(): lax.all_gather(local, group_axis)  376 us
    psum x2, waiting for transfers between devices, shards(): proj = lax.psum(partial_proj, 'row')  287 us
    psum x2, waiting for transfers between devices, shards(): lax.psum(jnp.dot(local_panel.T, local_panel, precision=highest, preferred...  281 us
    another operation x21, other arithmetic, shards(): lower = jnp.linalg.cholesky(gram)  114 us
    another operation x3, other arithmetic, shards(): lax.linalg.triangular_solve(lower, ident, left_side=True, lower=True)  59 us
    unnamed x28, local copies, waits for them, and re-layouts  55.2 us
    dot_general x2, matrix products, shards(): blocks = blocks - jnp.einsum('mb,bjt->mjt', basis, kept, precision=highest)  38.1 us
    dot_general x2, matrix products, shards(): partial_proj = jnp.einsum('mb,mjt->bjt', basis, blocks, precision=highest)  28.5 us
  transfers between devices with their start and end apart: 6, of which 6 were waited for; matrix products, arithmetic and copies ran while one was open for 1% of the time, Pallas kernels for 0%

profile of v1, /device:TPU:0, one launch (start us, length us, event | category | flops | bytes accessed | tf_op | source)
XLA Modules:
  0.0 1327.6 jit_solution(4765655790008969531)
XLA Ops:
  7.2 4.3 copy.28
  11.5 3.7 copy-done.2
  15.2 4.8 fusion.7
  20.7 141.6 %all-reduce.6.cloned.1.call-done = f32[384,384]{0,1:T(8,128)} async-done(((f32[384,384]{0,1:T(8,128)}), f32[384,384]{0,1:T(8,128)}) %all-reduce.6.cloned.1.call-update) | async-done | bytes 589840 | tf_op jit(solution)/shard_map/psum | solution.py:29
  162.3 1.3 copy.30
  164.7 11.7 cholesky.208
  176.4 9.8 custom-call.20
  186.9 11.7 cholesky.227
  198.6 10.0 custom-call.21
  209.1 11.7 cholesky.246
  224.2 6.4 while.4
  224.9 1.4 bitcast_dynamic-update-slice_fusion.4
  227.0 1.4 bitcast_dynamic-update-slice_fusion.4
  229.1 1.4 bitcast_dynamic-update-slice_fusion.4
  230.6 29.5 %custom-call.22 = f32[3,128,128]{1,2,0:T(8,128)S(1)} custom-call(f32[3,128,128]{2,1,0:T(8,128)S(1)} %get-tuple-element.18), custom_call_target="InvertDiagBlocksLowerTriangular" | custom-call | tf_op jit(solution)/shard_map/triangular_solve/custom-call.2 | solution.py:36
  261.9 7.0 fusion
  269.0 187.8 %all-gather.5.cloned.1.call-done = f32[12288,384]{0,1:T(8,128)} async-done(((f32[1536,384]{0,1:T(8,128)}), f32[12288,384]{0,1:T(8,128)}) %all-gather.5.cloned.1.call-update) | async-done | bytes 18874384 | tf_op jit(solution)/shard_map/all_gather | solution.py:11
  456.8 20.0 %copy.48 = f32[48,8,8,1536]{3,2,1,0:T(8,128)S(1)} copy(f32[48,8,8,1536]{3,1,2,0:T(8,128)} %bitcast.120) | data formatting | bytes 37748736
  476.8 5.2 bitcast_reduce_fusion
  482.1 1.4 copy-done.1
  483.5 13.0 fusion.4
  496.5 2.2 copy.31
  498.7 144.6 %all-reduce.8.cloned.1.call-done = f32[384,4,384]{2,0,1:T(8,128)} async-done(((f32[384,4,384]{2,0,1:T(8,128)}), f32[384,4,384]{2,0,1:T(8,128)}) %all-reduce.8.cloned.1.call-update) | async-done | bytes 2359312 | tf_op jit(solution)/shard_map/psum | solution.py:42
  643.3 21.4 %subtract_select_fusion.1 = f32[1536,4,384]{2,0,1:T(8,128)S(1)} fusion(f32[1536,384]{1,0:T(8,128)S(1)} %copy.31, pred[4]{0:T(512)(128)(4,1)S(1)} %get-tuple-element.69, f32[1536,384]{0,1:T(8,128)} %copy-done.1, f32[384,4,384]{2,0,1:T(8,128)} %all-reduce.8.cloned.1.call-done, pred[4]{0:T(512)(128)(4,1)S(1)} %get-tuple-element.68, f32[1536,4,384]{2,1,0:T(4,128)} %param.4), kind=kOutput, calls=%fused_computation.6 | convolution fusion | flops 10876944384 | bytes 25952264 | tf_op jit(solution)/shard_map/mb,bjt->mjt/dot_general | solution.py:44
  664.7 3.7 copy-done
  668.4 4.8 fusion.8
  673.5 139.6 %all-reduce.10.cloned.1.call-done = f32[384,384]{0,1:T(8,128)} async-done(((f32[384,384]{0,1:T(8,128)}), f32[384,384]{0,1:T(8,128)}) %all-reduce.10.cloned.1.call-update) | async-done | bytes 589840 | tf_op jit(solution)/shard_map/psum | solution.py:29
  813.1 1.3 copy.36
  815.6 11.7 cholesky.261
  827.4 9.8 custom-call.23
  837.8 11.7 cholesky.280
  850.9 10.2 custom-call.24
  861.5 11.7 cholesky.299
  876.7 6.4 while.5
  877.4 1.4 bitcast_dynamic-update-slice_fusion.5
  879.5 1.4 bitcast_dynamic-update-slice_fusion.5
  881.7 1.4 bitcast_dynamic-update-slice_fusion.5
  883.1 29.5 %custom-call.25 = f32[3,128,128]{1,2,0:T(8,128)S(1)} custom-call(f32[3,128,128]{2,1,0:T(8,128)S(1)} %get-tuple-element.19), custom_call_target="InvertDiagBlocksLowerTriangular" | custom-call | tf_op jit(solution)/shard_map/triangular_solve/custom-call.2 | solution.py:36
  914.5 6.9 convolution_select_fusion
  921.6 187.7 %all-gather.7.cloned.1.call-done = f32[12288,384]{1,0:T(8,128)} async-done(((f32[1536,384]{1,0:T(8,128)}), f32[12288,384]{1,0:T(8,128)}) %all-gather.7.cloned.1.call-update) | async-done | bytes 18874384 | tf_op jit(solution)/shard_map/all_gather | solution.py:11
  1109.3 7.5 reduce_sum.19
  1116.9 15.5 %fusion.1 = f32[384,4,384]{2,0,1:T(8,128)} fusion(f32[1536,4,384]{2,0,1:T(8,128)} %copy-done, f32[1536,384]{1,0:T(8,128)S(1)} %reduce_sum.19), kind=kOutput, calls=%fused_computation.13 | convolution fusion | flops 10871635968 | bytes 14155776 | tf_op jit(solution)/shard_map/mb,mjt->bjt/dot_general | solution.py:41
  1133.5 3.5 select_bitcast_fusion.1
  1137.2 142.1 %all-reduce.12.cloned.1.call-done = f32[384,4,384]{2,0,1:T(8,128)} async-done(((f32[384,4,384]{2,0,1:T(8,128)}), f32[384,4,384]{2,0,1:T(8,128)}) %all-reduce.12.cloned.1.call-update) | async-done | bytes 2359312 | tf_op jit(solution)/shard_map/psum | solution.py:42
  1279.3 2.1 select_bitcast_fusion
  1282.0 5.2 copy.41
  1287.2 16.8 %subtract_select_fusion = f32[1536,4,384]{2,0,1:T(8,128)S(1)} fusion(f32[1536,4,384]{2,0,1:T(8,128)S(1)} %bitcast.116, f32[1536,384]{1,0:T(8,128)S(1)} %reduce_sum.19, pred[4]{0:T(512)(128)(4,1)S(1)} %get-tuple-element.71, f32[384,4,384]{2,0,1:T(8,128)S(1)} %copy-done.3, pred[4]{0:T(512)(128)(4,1)S(1)} %get-tuple-element.70), kind=kOutput, calls=%fused_computation.5 | convolution fusion | flops 10876944384 | bytes 23592968 | tf_op jit(solution)/shard_map/mb,bjt->mjt/dot_general | solution.py:44
  1304.0 16.5 %copy.40 = f32[1536,4,384]{2,1,0:T(4,128)} copy(f32[1536,4,384]{2,0,1:T(8,128)S(1)} %subtract_select_fusion) | data formatting | bytes 18874368
  (96 shorter events, 19.8 us)
Async XLA Ops:
  7.2 155.1 %all-reduce.6.cloned.1.call-start = ((), (), s32[]{:S(2)}) async-start(), calls=%async_computation | async-start | bytes 1179648 | tf_op jit(solution)/shard_map/psum | solution.py:29
  11.5 3.7 copy-start.2
  20.1 436.7 %all-gather.5.cloned.1.call-start = ((), (), s32[]{:S(2)}) async-start(), calls=%async_computation.4 | async-start | bytes 21233664 | tf_op jit(solution)/shard_map/all_gather | solution.py:11
  268.9 374.4 %all-reduce.8.cloned.1.call-start = ((), (), s32[]{:S(2)}) async-start(), calls=%async_computation.1 | async-start | bytes 4718592 | tf_op jit(solution)/shard_map/psum | solution.py:42
  456.8 26.6 %slice-start.3 = ((s8[9437184]{0:T(1024)(128)(4,1)}), s8[4194304]{0:T(1024)(128)(4,1)S(1)}, s32[]{:S(2)}) async-start(s8[9437184]{0:T(1024)(128)(4,1)} %bitcast.117), calls=%async_computation.9 | async-start | bytes 8388608
  456.8 26.6 %slice-start.4 = ((s8[9437184]{0:T(1024)(128)(4,1)}), s8[4194304]{0:T(1024)(128)(4,1)S(1)}, s32[]{:S(2)}) async-start(s8[9437184]{0:T(1024)(128)(4,1)} %bitcast.117), calls=%async_computation.10 | async-start | bytes 8388608
  476.8 6.6 slice-start.5
  482.1 1.4 copy-start.1
  496.5 316.7 %all-reduce.10.cloned.1.call-start = ((), (), s32[]{:S(2)}) async-start(), calls=%async_computation.2 | async-start | bytes 1179648 | tf_op jit(solution)/shard_map/psum | solution.py:29
  664.7 3.7 copy-start
  673.3 436.0 %all-gather.7.cloned.1.call-start = ((), (), s32[]{:S(2)}) async-start(), calls=%async_computation.5 | async-start | bytes 21233664 | tf_op jit(solution)/shard_map/all_gather | solution.py:11
  921.4 357.8 %all-reduce.12.cloned.1.call-start = ((), (), s32[]{:S(2)}) async-start(), calls=%async_computation.3 | async-start | bytes 4718592 | tf_op jit(solution)/shard_map/psum | solution.py:42
  1133.5 3.5 copy-start.5
  1279.3 2.4 copy-start.4
  1281.6 5.6 slice-start
  1281.6 5.6 slice-start.1
  1282.0 5.3 slice-start.2
  1282.0 5.2 copy-start.3
Sparse Core Ops, SparseCore 0:
  20.2 141.9 all-reduce.5
  269.1 187.7 all-gather.4
  496.6 146.6 all-reduce.7
  673.4 139.6 all-reduce.9
  921.5 187.7 all-gather.6
  1132.5 146.6 all-reduce.11
